TPU v7x, 256 devices: a whole 4x4x8 slice. The times are simulated.
256 devices in a mesh: own: 32 (over x, z), row: 8 (over y, core).
Axes of the slice: x: 4, y: 4, z: 8, core: 2. Of those that a mesh axis runs over, the one named last changes fastest.
Arguments:
- sigma_anc: float32 [16384, 16384], P('row', 'own'), may hold values from -1.5 to 1.5
- row_blocks: int32 [64, 8], replicated, may hold values from 0 to 63, as said below
- panel1: float32 [64, 2048, 256], P('own', 'row'), may hold values from -0.375 to 0.375
- diag_inv1: float32 [64, 256, 256], P('own'), as said below
- mask1: int32 [64, 8], P('own', 'row'), may hold values 0 or 1
- parent_block2: float32 [64, 256, 256], P('own'), may hold values from -0.375 to 0.375
- panel2: float32 [64, 2048, 256], P('own', 'row'), may hold values from -0.375 to 0.375
- diag_inv2: float32 [64, 256, 256], P('own'), as said below
- mask2: int32 [64, 8], P('own', 'row'), may hold values 0 or 1
Outputs:
- sel1_panel: float32 [64, 2048, 256], P('own', 'row')
- sel1_diag: float32 [64, 256, 256], P('own')
- sel2_parent: float32 [64, 256, 256], P('own')
- sel2_panel: float32 [64, 2048, 256], P('own', 'row')
- sel2_diag: float32 [64, 256, 256], P('own')
Inputs may be any that keep to these rules, and one draw needn't show every extreme that they name: `row_blocks`: entry l of each row lies in block rows 8 * l to 8 * (l + 1) - 1; for supernodes s with the same s // 2, the entries of one column l lie in different aligned runs of 2 block rows. `diag_inv1`: lower triangular, with diagonal entries from 1 to 2. `diag_inv2`: lower triangular, with diagonal entries from 1 to 2.
All inputs are finite; a program needn't handle non-finite values. No bound on the sum of `mask1` or of `mask2` on one device may be relied on, other than what follows from the above.
Results may differ from a plain program's by a relative error of at most 0.000071.
Values sent between devices are 32-bit elements; how exact they have to be, the bound alone decides.
No kernel may reach another device: no remote copies, remote signals or barrier semaphores. Data moves between devices by JAX's collectives and lax.ppermute only.
A program may use at most 128 MiB of HBM per device.

v0:
```python
import jax
import jax.numpy as jnp
from jax import lax
from jax.sharding import PartitionSpec as P

B = 256
HIGH = lax.Precision.HIGHEST


def shifted(shard, axis, by):
    length = lax.axis_size(axis)
    return lax.ppermute(shard, axis, [(i, (i + by) % length) for i in range(length)])


def product(form, left, right):
    return jnp.einsum(form, left, right, precision=HIGH)


def select_send(sigma_local, row_blocks, slots):
    own_count = lax.axis_size("own")
    own_here = lax.axis_index("own")
    row_here = lax.axis_index("row")
    rows_here = sigma_local.shape[0] // B
    cols_here = sigma_local.shape[1] // B
    rowlist = row_blocks.reshape(own_count, slots, -1)
    group = own_here * cols_here // rows_here
    want_col = lax.dynamic_index_in_dim(rowlist, group, 2, keepdims=False)
    local_col = want_col - own_here * cols_here
    match = ((local_col >= 0) & (local_col < cols_here)).astype(jnp.int32)
    which = jnp.sum(match * jnp.arange(slots, dtype=jnp.int32)[None, :], axis=1)
    chosen = rowlist[jnp.arange(own_count, dtype=jnp.int32), which]
    chosen_row = (
        lax.dynamic_index_in_dim(chosen, row_here, 1, keepdims=False) - row_here * rows_here
    )
    chosen_col = jnp.clip(
        lax.dynamic_index_in_dim(chosen, group, 1, keepdims=False) - own_here * cols_here,
        0,
        cols_here - 1,
    )
    blocks4 = sigma_local.reshape(rows_here, B, cols_here, B)
    return blocks4[chosen_row, :, chosen_col, :]


def select_take(received, row_blocks, slots, cols_here):
    mine = lax.axis_index("own") * slots + jnp.arange(slots, dtype=jnp.int32)
    rowlist = row_blocks[mine]
    sender = rowlist // cols_here
    return received[sender]


def on_device(
    sigma_anc, row_blocks, panel1, diag_inv1, mask1, parent_block2, panel2, diag_inv2, mask2
):
    slots = panel1.shape[0]
    cols_here = sigma_anc.shape[1] // B
    keep_own2 = mask2.astype(jnp.float32)
    up_parent = product("kij,kjc->kic", parent_block2, diag_inv2)
    factor2_own = keep_own2[:, :, None] * product("kij,kjc->kic", panel2, diag_inv2)
    factor2_child = shifted(factor2_own, "own", -1)
    outgoing = select_send(sigma_anc, row_blocks, slots)
    received = lax.all_to_all(outgoing, "own", split_axis=0, concat_axis=0, tiled=True)
    blocks1 = select_take(received, row_blocks, slots, cols_here)
    keep1 = mask1.astype(jnp.float32)
    factor1 = keep1[:, :, None] * product("kij,kjc->kic", panel1, diag_inv1)
    factors1 = lax.all_gather(factor1, "row", axis=1, tiled=True).reshape(slots, -1, B, B)
    sel1_panel = -keep1[:, :, None] * product("kmij,kmjc->kic", blocks1, factors1)
    gram1 = product("kji,kjc->kic", diag_inv1, diag_inv1)
    sel1_diag = gram1 - lax.psum(product("kji,kjc->kic", factor1, sel1_panel), "row")
    factor2 = keep1[:, :, None] * factor2_child
    factors2 = lax.all_gather(factor2, "row", axis=1, tiled=True).reshape(slots, -1, B, B)
    anc2 = keep1[:, :, None] * product("kmij,kmjc->kic", blocks1, factors2)
    par_panel = shifted(sel1_panel, "own", 1)
    par_anc = shifted(anc2, "own", 1)
    par_diag = shifted(sel1_diag, "own", 1)
    sel2_panel = -keep_own2[:, :, None] * (product("kij,kjc->kic", par_panel, up_parent) + par_anc)
    cross = product("kji,kjc->kic", par_panel, factor2_own)
    back = product("kji,kjc->kic", factor2_own, sel2_panel)
    par_diag, cross, back = lax.optimization_barrier((par_diag, cross, back))
    cross, back = lax.psum((cross, back), "row")
    sel2_parent = -(product("kij,kjc->kic", par_diag, up_parent) + cross)
    gram2 = product("kji,kjc->kic", diag_inv2, diag_inv2)
    sel2_diag = gram2 - product("kji,kjc->kic", up_parent, sel2_parent) - back
    return (sel1_panel, sel1_diag, sel2_parent, sel2_panel, sel2_diag)


def solution(mesh):
    in_specs = (
        P("row", "own"),
        P(),
        P("own", "row", None),
        P("own", None, None),
        P("own", "row"),
        P("own", None, None),
        P("own", "row", None),
        P("own", None, None),
        P("own", "row"),
    )
    out_specs = (
        P("own", "row", None),
        P("own", None, None),
        P("own", None, None),
        P("own", "row", None),
        P("own", None, None),
    )
    return jax.shard_map(
        on_device, mesh=mesh, in_specs=in_specs, out_specs=out_specs, check_vma=False
    )
```

profile of v0, /device:TPU:2, one launch (start us, length us, event | category | flops | bytes accessed | tf_op | source)
XLA Modules:
  0.0 444.9 jit_solution(6164868798614665549)
XLA Ops:
  7.2 0.0 copy-start
  7.2 0.8 copy.67
  8.0 0.1 constant_dynamic-slice_fusion
  8.1 0.1 copy.90
  8.2 0.1 copy.69
  8.3 0.1 fusion.7
  8.5 0.7 gather_fusion
  9.1 5.9 %reshape.167 = f32[8,256,2,256]{3,2,1,0:T(2,128)} reshape(f32[2048,512]{1,0:T(8,128)} %param.9) | data formatting | bytes 8388608 | tf_op jit(solution)/shard_map/reshape | solution.py:40
  15.1 4.7 %copy.72 = f32[8,256,2,256]{3,1,2,0:T(8,128)} copy(f32[8,256,2,256]{3,2,1,0:T(2,128)} %reshape.167) | data formatting | bytes 8388608 | tf_op jit(solution)/shard_map/reshape | solution.py:40
  19.7 0.2 fusion.11
  19.9 6.5 %gather_fusion.1 = f32[32,256,256]{2,1,0:T(8,128)} fusion(f32[8,256,2,256]{3,1,2,0:T(8,128)} %copy.72, s32[32]{0:T(128)S(1)} %fusion.11), kind=kCustom, calls=%fused_computation.1 | custom fusion | bytes 16777472 | tf_op jit(solution)/shard_map/gather | solution.py:41
  26.5 11.8 %all-to-all-start = ((f32[32,256,256]{2,1,0:T(8,128)}), f32[32,256,256]{2,1,0:T(8,128)}, u32[]{:S(2)}, u32[]{:S(2)}) async-start(f32[32,256,256]{2,1,0:T(8,128)} %gather_fusion.1), calls=%async_computation | async-start | bytes 16777216 | tf_op jit(solution)/shard_map/all_to_all | solution.py:61
  38.3 0.0 all-gather.3.cloned.1.call-start
  38.4 1.5 convolution_multiply_fusion.1
  39.8 0.0 all-gather.3.cloned.1.call-update
  39.8 0.0 all-gather.5.cloned.1.call-start
  39.9 0.7 convolution_multiply_fusion
  40.6 2.8 collective-permute-start.2
  43.3 190.9 %collective-permute-done.2 = f32[2,256,256]{2,1,0:T(8,128)S(1)} collective-permute-done((f32[2,256,256]{2,1,0:T(8,128)S(1)}, f32[2,256,256]{2,1,0:T(8,128)S(1)}, u32[]{:S(2)}, u32[]{:S(2)}) %collective-permute-start.2) | collective-permute-done | bytes 524320 | tf_op jit(solution)/shard_map/ppermute | solution.py:12
  234.2 0.9 broadcast_multiply_fusion
  235.1 0.0 all-gather.5.cloned.1.call-update
  235.1 0.0 all-reduce.4.cloned.1.call-start
  235.2 0.6 gather_fusion.2
  235.8 0.1 reshape.158
  235.9 6.2 %gather_fusion.3 = f32[16,256,256]{2,1,0:T(8,128)} fusion(f32[32,256,256]{2,1,0:T(8,128)} %all-to-all-done, s32[1024]{0:T(1024)S(1)} %pad_clamp_fusion), kind=kCustom, calls=%fused_computation.3 | custom fusion | bytes 8388672 | tf_op jit(solution)/shard_map/gather | solution.py:48
  242.1 8.1 %fusion.3 = f32[2,256,256]{2,1,0:T(8,128)S(1)} fusion(f32[2,8,256,256]{3,2,1,0:T(8,128)} %bitcast.67, f32[2,8,256,256]{3,2,1,0:T(8,128)} %bitcast.69, f32[2]{0:T(128)S(1)} %fusion.16), kind=kOutput, calls=%fused_computation.14 | convolution fusion | flops 3221356544 | bytes 8912904 | tf_op jit(solution)/shard_map/kmij,kmjc->kic/dot_general | solution.py:16
  250.2 0.0 copy-start.3
  250.2 0.3 collective-permute-start.1
  250.5 1.9 fusion.18
  252.4 21.4 %all-gather.5.cloned.1.call-done = f32[2,2048,256]{2,1,0:T(8,128)} async-done(((f32[2,256,256]{2,1,0:T(8,128)}), f32[2,2048,256]{2,1,0:T(8,128)}) %all-gather.5.cloned.1.call-update) | async-done | bytes 4194320 | tf_op jit(solution)/shard_map/all_gather | solution.py:70
  273.8 8.2 %fusion.1 = f32[2,256,256]{2,1,0:T(8,128)} fusion(f32[2,8,256,256]{3,2,1,0:T(8,128)} %bitcast.68, f32[2,8,256,256]{3,2,1,0:T(8,128)} %bitcast.70, f32[2]{0:T(128)S(1)} %convert_bitcast_fusion.1), kind=kOutput, calls=%fused_computation.8 | convolution fusion | flops 3221356544 | bytes 8912904 | tf_op jit(solution)/shard_map/kmij,kmjc->kic/dot_general | solution.py:16
  282.0 1.5 collective-permute-start.3
  283.6 0.0 all-reduce.4.cloned.1.call-update
  283.6 0.0 all-reduce.6.cloned.1.call-start
  283.7 1.7 fusion.20
  285.4 63.5 %all-reduce.4.cloned.1.call-done = f32[2,256,256]{2,1,0:T(8,128)} async-done(((f32[2,256,256]{2,1,0:T(8,128)}), f32[2,256,256]{2,1,0:T(8,128)}) %all-reduce.4.cloned.1.call-update) | async-done | bytes 524304 | tf_op jit(solution)/shard_map/psum | solution.py:68
  348.9 2.9 convolution_subtract_fusion.1
  351.8 1.6 collective-permute-start
  353.3 1.7 fusion.2
  355.0 1.8 fusion.21
  356.9 1.8 fusion.19
  358.7 7.1 %collective-permute-done = f32[2,256,256]{2,1,0:T(8,128)} collective-permute-done((f32[2,256,256]{2,1,0:T(8,128)}, f32[2,256,256]{2,1,0:T(8,128)}, u32[]{:S(2)}, u32[]{:S(2)}) %collective-permute-start) | collective-permute-done | bytes 524320 | tf_op jit(solution)/shard_map/ppermute | solution.py:12
  365.8 0.0 all-reduce.6.cloned.1.call-update
  365.8 1.1 fusion.22
  366.9 67.6 %all-reduce.6.cloned.1.call-done = (f32[2,256,256]{2,1,0:T(8,128)}, f32[2,256,256]{2,1,0:T(8,128)}) async-done(((f32[2,256,256]{2,1,0:T(8,128)}, f32[2,256,256]{2,1,0:T(8,128)}), (f32[2,256,256]{2,1,0:T(8,128)}, f32[2,256,256]{2,1,0:T(8,128)})) %all-reduce.6.cloned.1.call-update) | async-done | bytes 1048592 | tf_op jit(solution)/shard_map/psum | solution.py:79
  434.5 1.9 fusion
  436.4 1.0 convolution_subtract_fusion
  437.5 0.9 sub.48
  (33 shorter events, 0.1 us)
Async XLA Ops:
  7.2 32.7 %copy-start = (f32[2,256,256]{2,1,0:T(8,128)S(1)}, f32[2,256,256]{2,1,0:T(8,128)}, u32[]{:S(2)}) copy-start(f32[2,256,256]{2,1,0:T(8,128)} %param.16) | copy-start | bytes 1572868
  26.4 11.9 %copy-start.9 = (s32[2,1]{0,1:T(1,128)S(1)}, s32[2,1]{0,1:T(1,128)}, u32[]{:S(2)}) copy-start(s32[2,1]{0,1:T(1,128)} %param.13) | copy-start | bytes 28
  26.4 11.9 %copy-start.2 = (f32[2,256,256]{2,1,0:T(8,128)S(1)}, f32[2,256,256]{2,1,0:T(8,128)}, u32[]{:S(2)}) copy-start(f32[2,256,256]{2,1,0:T(8,128)} %param.12) | copy-start | bytes 1572868
  26.4 11.9 %copy-start.7 = (f32[2,256,256]{2,1,0:T(8,128)S(1)}, f32[2,256,256]{2,1,0:T(8,128)}, u32[]{:S(2)}) copy-start(f32[2,256,256]{2,1,0:T(8,128)} %param.11) | copy-start | bytes 1572868
  26.4 13.5 %copy-start.10 = (s32[2,1]{0,1:T(1,128)S(1)}, s32[2,1]{0,1:T(1,128)}, u32[]{:S(2)}) copy-start(s32[2,1]{0,1:T(1,128)} %param.17) | copy-start | bytes 28
  26.4 13.5 %copy-start.8 = (f32[2,256,256]{2,1,0:T(8,128)S(1)}, f32[2,256,256]{2,1,0:T(8,128)}, u32[]{:S(2)}) copy-start(f32[2,256,256]{2,1,0:T(8,128)} %param.15) | copy-start | bytes 1572868
  26.5 209.4 %all-to-all-start = ((f32[32,256,256]{2,1,0:T(8,128)}), f32[32,256,256]{2,1,0:T(8,128)}, u32[]{:S(2)}, u32[]{:S(2)}) async-start(f32[32,256,256]{2,1,0:T(8,128)} %gather_fusion.1), calls=%async_computation | async-start | bytes 16777216 | tf_op jit(solution)/shard_map/all_to_all | solution.py:61
  38.3 203.8 %all-gather.3.cloned.1.call-start = ((), (), s32[]{:S(2)}) async-start(), calls=%async_computation.1 | async-start | bytes 4718592 | tf_op jit(solution)/shard_map/all_gather | solution.py:65
  39.8 234.0 %all-gather.5.cloned.1.call-start = ((), (), s32[]{:S(2)}) async-start(), calls=%async_computation.3 | async-start | bytes 4718592 | tf_op jit(solution)/shard_map/all_gather | solution.py:70
  40.6 193.6 %collective-permute-start.2 = (f32[2,256,256]{2,1,0:T(8,128)S(1)}, f32[2,256,256]{2,1,0:T(8,128)S(1)}, u32[]{:S(2)}, u32[]{:S(2)}) collective-permute-start(f32[2,256,256]{2,1,0:T(8,128)S(1)} %convolution_multiply_fusion), channel_id=1, source_target_pairs={{0,248},{8,0},{16,8},{24,16},{32,24},{40,32},{48,40},{56,48},{64,5... | collective-permute-start | bytes 1572872 | tf_op jit(solution)/shard_map/ppermute | solution.py:12
  235.1 113.7 %all-reduce.4.cloned.1.call-start = ((), (), s32[]{:S(2)}) async-start(), calls=%async_computation.2 | async-start | bytes 1048576 | tf_op jit(solution)/shard_map/psum | solution.py:68
  242.1 8.4 %copy-start.1 = (f32[2,256,256]{2,1,0:T(8,128)S(1)}, f32[2,256,256]{2,1,0:T(8,128)}, u32[]{:S(2)}) copy-start(f32[2,256,256]{2,1,0:T(8,128)} %convolution_multiply_fusion.1) | copy-start | bytes 1572868
  250.2 31.8 %copy-start.3 = (f32[2,256,256]{2,1,0:T(8,128)}, f32[2,256,256]{2,1,0:T(8,128)S(1)}, u32[]{:S(2)}) copy-start(f32[2,256,256]{2,1,0:T(8,128)S(1)} %fusion.3) | copy-start | bytes 1572868
  250.2 103.1 %collective-permute-start.1 = (f32[2,256,256]{2,1,0:T(8,128)S(1)}, f32[2,256,256]{2,1,0:T(8,128)S(1)}, u32[]{:S(2)}, u32[]{:S(2)}) collective-permute-start(f32[2,256,256]{2,1,0:T(8,128)S(1)} %fusion.3), channel_id=1, source_target_pairs={{0,8},{8,16},{16,24},{24,32},{32,40},{40,48},{48,56},{56,64},{64,7... | collective-permute-start | bytes 1572872 | tf_op jit(solution)/shard_map/ppermute | solution.py:12
  282.0 71.3 %collective-permute-start.3 = (f32[2,256,256]{2,1,0:T(8,128)}, f32[2,256,256]{2,1,0:T(8,128)}, u32[]{:S(2)}, u32[]{:S(2)}) collective-permute-start(f32[2,256,256]{2,1,0:T(8,128)} %fusion.1), channel_id=1, source_target_pairs={{0,8},{8,16},{16,24},{24,32},{32,40},{40,48},{48,56},{56,64},{64,7... | collective-permute-start | bytes 1572872 | tf_op jit(solution)/shard_map/ppermute | solution.py:12
  283.6 150.9 %all-reduce.6.cloned.1.call-start = ((), (), s32[]{:S(2)}) async-start(), calls=%async_computation.4 | async-start | bytes 2097152 | tf_op jit(solution)/shard_map/psum | solution.py:79
  351.8 14.1 %collective-permute-start = (f32[2,256,256]{2,1,0:T(8,128)}, f32[2,256,256]{2,1,0:T(8,128)}, u32[]{:S(2)}, u32[]{:S(2)}) collective-permute-start(f32[2,256,256]{2,1,0:T(8,128)} %convolution_subtract_fusion.1), channel_id=1, source_target_pairs={{0,8},{8,16},{16,24},{24,32},{32,40},{40,48},{48,56},{56,64},{64,7... | collective-permute-start | bytes 1572872 | tf_op jit(solution)/shard_map/ppermute | solution.py:12
  355.0 82.5 %copy-start.4 = (f32[2,256,256]{2,1,0:T(8,128)}, f32[2,256,256]{2,1,0:T(8,128)S(1)}, u32[]{:S(2)}) copy-start(f32[2,256,256]{2,1,0:T(8,128)S(1)} %fusion.2) | copy-start | bytes 1572868
  434.5 3.0 copy-start.6
  436.4 2.0 copy-start.5
Sparse Core Ops, SparseCore 0:
  41.5 35.7 all-gather.2
  235.3 38.5 all-gather.4
  283.7 65.0 all-reduce.3
  366.0 68.4 all-reduce.5
where the time goes:
time: 445 us
  waiting for transfers between devices  351 us (79%)
  matrix products  34.3 us (8%)
  local copies, waits for them, and re-layouts  25.7 us (6%)
  starting transfers between devices  18.1 us (4%)
  between operations  14 us (3%)
    ppermute x4, waiting for transfers between devices, shifted(): lax.ppermute(shard, axis, [(i, (i + by) % length) for i in range(length)])  198 us
    psum x1, waiting for transfers between devices, on_device(): cross, back = lax.psum((cross, back), 'row')  67.6 us
    psum x1, waiting for transfers between devices, on_device(): lax.psum(product('kji,kjc->kic', factor1, sel1_panel), 'row')  63.5 us
    dot_general x13, matrix products, product(): return jnp.einsum(form, left, right, precision=HIGH)  34.3 us
    all_gather x1, waiting for transfers between devices, on_device(): lax.all_gather(factor2, 'row', axis=1, tiled=True).reshape(slots, -1, B, B)  21.4 us
    all_to_all x1, starting transfers between devices, on_device(): lax.all_to_all(outgoing, 'own', split_axis=0, concat_axis=0, tiled=True)  11.8 us
    reshape x2, local copies, waits for them, and re-layouts, select_send(): blocks4 = sigma_local.reshape(rows_here, B, cols_here, B)  10.6 us
  transfers between devices with their start and end apart: 9, of which 5 were waited for; matrix products, arithmetic and copies ran while one was open for 9% of the time, Pallas kernels for 0%

commit v1 on v0

--- a/solution.py
+++ b/solution.py
@@ -65,7 +65,9 @@
     factors1 = lax.all_gather(factor1, "row", axis=1, tiled=True).reshape(slots, -1, B, B)
     sel1_panel = -keep1[:, :, None] * product("kmij,kmjc->kic", blocks1, factors1)
     gram1 = product("kji,kjc->kic", diag_inv1, diag_inv1)
-    sel1_diag = gram1 - lax.psum(product("kji,kjc->kic", factor1, sel1_panel), "row")
+    sel1_diag = gram1 - jnp.sum(
+        lax.all_gather(product("kji,kjc->kic", factor1, sel1_panel), "row"), axis=0
+    )
     factor2 = keep1[:, :, None] * factor2_child
     factors2 = lax.all_gather(factor2, "row", axis=1, tiled=True).reshape(slots, -1, B, B)
     anc2 = keep1[:, :, None] * product("kmij,kmjc->kic", blocks1, factors2)

time: 445 us -> 411 us (0.924)
  waiting for transfers between devices: 351 us -> 314 us
    psum x1 -> x0, waiting for transfers between devices: 63.5 us -> none  [on_device(): lax.psum(product('kji,kjc->kic', factor1, sel1_panel), 'row')]
    ppermute x4, waiting for transfers between devices: 198 us -> 226 us  [shifted(): lax.ppermute(shard, axis, [(i, (i + by) % length) for i in range(length)])]
  transfers between devices with their start and end apart: 9 -> 9, of which waited for: 5 -> 7; matrix products, arithmetic and copies ran while one was open for 9% -> 8% of each run, Pallas kernels for 0% -> 0%
where the time goes in v1:
time: 411 us
  waiting for transfers between devices  314 us (76%)
  matrix products  32 us (8%)
  local copies, waits for them, and re-layouts  25.7 us (6%)
  starting transfers between devices  19.6 us (5%)
  between operations  14 us (3%)
  other arithmetic  5.45 us (1%)
    ppermute x4, waiting for transfers between devices, shifted(): lax.ppermute(shard, axis, [(i, (i + by) % length) for i in range(length)])  226 us
    psum x1, waiting for transfers between devices, on_device(): cross, back = lax.psum((cross, back), 'row')  65.9 us
    dot_general x13, matrix products, product(): return jnp.einsum(form, left, right, precision=HIGH)  32 us
    all_gather x1, waiting for transfers between devices, on_device(): lax.all_gather(factor2, 'row', axis=1, tiled=True).reshape(slots, -1, B, B)  21.6 us
    all_to_all x1, starting transfers between devices, on_device(): lax.all_to_all(outgoing, 'own', split_axis=0, concat_axis=0, tiled=True)  11.8 us
    reshape x2, local copies, waits for them, and re-layouts, select_send(): blocks4 = sigma_local.reshape(rows_here, B, cols_here, B)  10.6 us
  transfers between devices with their start and end apart: 9, of which 7 were waited for; matrix products, arithmetic and copies ran while one was open for 8% of the time, Pallas kernels for 0%

profile of v1, /device:TPU:2, one launch (start us, length us, event | category | flops | bytes accessed | tf_op | source)
XLA Modules:
  0.0 410.7 jit_solution(14497119657009376390)
XLA Ops:
  7.2 0.8 copy.81
  8.0 0.1 constant_dynamic-slice_fusion
  8.1 0.1 copy.104
  8.2 0.1 copy.83
  8.3 0.1 fusion.7
  8.5 0.7 gather_fusion
  9.1 5.9 %reshape.168 = f32[8,256,2,256]{3,2,1,0:T(2,128)} reshape(f32[2048,512]{1,0:T(8,128)} %param.9) | data formatting | bytes 8388608 | tf_op jit(solution)/shard_map/reshape | solution.py:40
  15.1 4.6 %copy.86 = f32[8,256,2,256]{3,1,2,0:T(8,128)} copy(f32[8,256,2,256]{3,2,1,0:T(2,128)} %reshape.168) | data formatting | bytes 8388608 | tf_op jit(solution)/shard_map/reshape | solution.py:40
  19.7 0.2 fusion.11
  19.9 6.5 %gather_fusion.1 = f32[32,256,256]{2,1,0:T(8,128)} fusion(f32[8,256,2,256]{3,1,2,0:T(8,128)} %copy.86, s32[32]{0:T(128)S(1)} %fusion.11), kind=kCustom, calls=%fused_computation.1 | custom fusion | bytes 16777472 | tf_op jit(solution)/shard_map/gather | solution.py:41
  26.4 11.8 %all-to-all-start = ((f32[32,256,256]{2,1,0:T(8,128)}), f32[32,256,256]{2,1,0:T(8,128)}, u32[]{:S(2)}, u32[]{:S(2)}) async-start(f32[32,256,256]{2,1,0:T(8,128)} %gather_fusion.1), calls=%async_computation | async-start | bytes 16777216 | tf_op jit(solution)/shard_map/all_to_all | solution.py:61
  38.3 0.0 all-gather.5.cloned.1.call-start
  38.4 1.5 convolution_multiply_fusion.1
  39.8 0.0 all-gather.5.cloned.1.call-update
  39.8 0.0 all-gather.7.cloned.1.call-start
  39.9 0.7 convolution_multiply_fusion
  40.6 2.7 collective-permute-start.2
  43.3 190.9 %collective-permute-done.2 = f32[2,256,256]{2,1,0:T(8,128)S(1)} collective-permute-done((f32[2,256,256]{2,1,0:T(8,128)S(1)}, f32[2,256,256]{2,1,0:T(8,128)S(1)}, u32[]{:S(2)}, u32[]{:S(2)}) %collective-permute-start.2) | collective-permute-done | bytes 524320 | tf_op jit(solution)/shard_map/ppermute | solution.py:12
  234.2 0.9 broadcast_multiply_fusion
  235.1 0.0 all-gather.7.cloned.1.call-update
  235.1 0.0 all-gather.9.cloned.1.call-start
  235.2 0.6 gather_fusion.2
  235.8 0.1 reshape.158
  235.9 6.2 %gather_fusion.3 = f32[16,256,256]{2,1,0:T(8,128)} fusion(f32[32,256,256]{2,1,0:T(8,128)} %all-to-all-done, s32[1024]{0:T(1024)S(1)} %pad_clamp_fusion), kind=kCustom, calls=%fused_computation.3 | custom fusion | bytes 8388672 | tf_op jit(solution)/shard_map/gather | solution.py:48
  242.1 8.1 %fusion.3 = f32[2,256,256]{2,1,0:T(8,128)S(1)} fusion(f32[2,8,256,256]{3,2,1,0:T(8,128)} %bitcast.68, f32[2,8,256,256]{3,2,1,0:T(8,128)} %bitcast.71, f32[2]{0:T(128)S(1)} %fusion.16), kind=kOutput, calls=%fused_computation.14 | convolution fusion | flops 3221356544 | bytes 8912904 | tf_op jit(solution)/shard_map/kmij,kmjc->kic/dot_general | solution.py:16
  250.2 1.9 fusion.18
  252.1 0.0 all-reduce.3.cloned.1.call-start
  252.2 21.6 %all-gather.7.cloned.1.call-done = f32[2,2048,256]{2,1,0:T(8,128)} async-done(((f32[2,256,256]{2,1,0:T(8,128)}), f32[2,2048,256]{2,1,0:T(8,128)}) %all-gather.7.cloned.1.call-update) | async-done | bytes 4194320 | tf_op jit(solution)/shard_map/all_gather | solution.py:72
  273.8 8.1 %fusion.1 = f32[2,256,256]{2,1,0:T(8,128)S(1)} fusion(f32[2,8,256,256]{3,2,1,0:T(8,128)} %bitcast.69, f32[2,8,256,256]{3,2,1,0:T(8,128)} %bitcast.72, f32[2]{0:T(128)S(1)} %convert_bitcast_fusion.1), kind=kOutput, calls=%fused_computation.8 | convolution fusion | flops 3221356544 | bytes 8912904 | tf_op jit(solution)/shard_map/kmij,kmjc->kic/dot_general | solution.py:16
  281.9 1.8 collective-permute-start.3
  283.8 1.6 collective-permute-start.1
  285.3 0.7 fusion.20
  286.0 13.1 %collective-permute-done.3 = f32[2,256,256]{2,1,0:T(8,128)S(1)} collective-permute-done((f32[2,256,256]{2,1,0:T(8,128)S(1)}, f32[2,256,256]{2,1,0:T(8,128)S(1)}, u32[]{:S(2)}, u32[]{:S(2)}) %collective-permute-start.3) | collective-permute-done | bytes 524320 | tf_op jit(solution)/shard_map/ppermute | solution.py:12
  299.1 10.6 %collective-permute-done.1 = f32[2,256,256]{2,1,0:T(8,128)S(1)} collective-permute-done((f32[2,256,256]{2,1,0:T(8,128)S(1)}, f32[2,256,256]{2,1,0:T(8,128)S(1)}, u32[]{:S(2)}, u32[]{:S(2)}) %collective-permute-start.1) | collective-permute-done | bytes 524320 | tf_op jit(solution)/shard_map/ppermute | solution.py:12
  309.6 0.7 fusion.2
  310.3 0.6 all-gather.9.cloned.1.call-done
  310.9 3.3 reduce_sum.22
  314.2 2.9 convolution_subtract_fusion.1
  317.1 1.6 collective-permute-start
  318.7 1.8 fusion.21
  320.5 1.8 fusion.19
  322.4 11.2 %collective-permute-done = f32[2,256,256]{2,1,0:T(8,128)S(1)} collective-permute-done((f32[2,256,256]{2,1,0:T(8,128)}, f32[2,256,256]{2,1,0:T(8,128)S(1)}, u32[]{:S(2)}, u32[]{:S(2)}) %collective-permute-start) | collective-permute-done | bytes 524320 | tf_op jit(solution)/shard_map/ppermute | solution.py:12
  333.5 0.0 all-reduce.3.cloned.1.call-update
  333.5 1.1 fusion.22
  334.6 65.9 %all-reduce.3.cloned.1.call-done = (f32[2,256,256]{2,1,0:T(8,128)}, f32[2,256,256]{2,1,0:T(8,128)}) async-done(((f32[2,256,256]{2,1,0:T(8,128)}, f32[2,256,256]{2,1,0:T(8,128)}), (f32[2,256,256]{2,1,0:T(8,128)}, f32[2,256,256]{2,1,0:T(8,128)})) %all-reduce.3.cloned.1.call-update) | async-done | bytes 1048592 | tf_op jit(solution)/shard_map/psum | solution.py:81
  400.5 1.8 fusion
  402.3 1.0 convolution_subtract_fusion
  403.3 0.9 sub.48
  (36 shorter events, 0.2 us)
Async XLA Ops:
  7.2 32.7 %copy-start = (f32[2,256,256]{2,1,0:T(8,128)S(1)}, f32[2,256,256]{2,1,0:T(8,128)}, u32[]{:S(2)}) copy-start(f32[2,256,256]{2,1,0:T(8,128)} %param.16) | copy-start | bytes 1572868
  26.4 11.9 %copy-start.10 = (s32[2,1]{0,1:T(1,128)S(1)}, s32[2,1]{0,1:T(1,128)}, u32[]{:S(2)}) copy-start(s32[2,1]{0,1:T(1,128)} %param.13) | copy-start | bytes 28
  26.4 11.9 %copy-start.2 = (f32[2,256,256]{2,1,0:T(8,128)S(1)}, f32[2,256,256]{2,1,0:T(8,128)}, u32[]{:S(2)}) copy-start(f32[2,256,256]{2,1,0:T(8,128)} %param.12) | copy-start | bytes 1572868
  26.4 11.9 %copy-start.8 = (f32[2,256,256]{2,1,0:T(8,128)S(1)}, f32[2,256,256]{2,1,0:T(8,128)}, u32[]{:S(2)}) copy-start(f32[2,256,256]{2,1,0:T(8,128)} %param.11) | copy-start | bytes 1572868
  26.4 13.5 %copy-start.11 = (s32[2,1]{0,1:T(1,128)S(1)}, s32[2,1]{0,1:T(1,128)}, u32[]{:S(2)}) copy-start(s32[2,1]{0,1:T(1,128)} %param.17) | copy-start | bytes 28
  26.4 13.5 %copy-start.9 = (f32[2,256,256]{2,1,0:T(8,128)S(1)}, f32[2,256,256]{2,1,0:T(8,128)}, u32[]{:S(2)}) copy-start(f32[2,256,256]{2,1,0:T(8,128)} %param.15) | copy-start | bytes 1572868
  26.4 209.4 %all-to-all-start = ((f32[32,256,256]{2,1,0:T(8,128)}), f32[32,256,256]{2,1,0:T(8,128)}, u32[]{:S(2)}, u32[]{:S(2)}) async-start(f32[32,256,256]{2,1,0:T(8,128)} %gather_fusion.1), calls=%async_computation | async-start | bytes 16777216 | tf_op jit(solution)/shard_map/all_to_all | solution.py:61
  38.3 203.8 %all-gather.5.cloned.1.call-start = ((), (), s32[]{:S(2)}) async-start(), calls=%async_computation.1 | async-start | bytes 4718592 | tf_op jit(solution)/shard_map/all_gather | solution.py:65
  39.8 234.0 %all-gather.7.cloned.1.call-start = ((), (), s32[]{:S(2)}) async-start(), calls=%async_computation.2 | async-start | bytes 4718592 | tf_op jit(solution)/shard_map/all_gather | solution.py:72
  40.6 193.6 %collective-permute-start.2 = (f32[2,256,256]{2,1,0:T(8,128)S(1)}, f32[2,256,256]{2,1,0:T(8,128)S(1)}, u32[]{:S(2)}, u32[]{:S(2)}) collective-permute-start(f32[2,256,256]{2,1,0:T(8,128)S(1)} %convolution_multiply_fusion), channel_id=1, source_target_pairs={{0,248},{8,0},{16,8},{24,16},{32,24},{40,32},{48,40},{56,48},{64,5... | collective-permute-start | bytes 1572872 | tf_op jit(solution)/shard_map/ppermute | solution.py:12
  235.1 75.8 %all-gather.9.cloned.1.call-start = ((), (), s32[]{:S(2)}) async-start(), calls=%async_computation.3 | async-start | bytes 4718592 | tf_op jit(solution)/shard_map/all_gather | solution.py:69
  242.1 8.1 %copy-start.1 = (f32[2,256,256]{2,1,0:T(8,128)S(1)}, f32[2,256,256]{2,1,0:T(8,128)}, u32[]{:S(2)}) copy-start(f32[2,256,256]{2,1,0:T(8,128)} %convolution_multiply_fusion.1) | copy-start | bytes 1572868
  250.2 33.5 %copy-start.3 = (f32[2,256,256]{2,1,0:T(8,128)}, f32[2,256,256]{2,1,0:T(8,128)S(1)}, u32[]{:S(2)}) copy-start(f32[2,256,256]{2,1,0:T(8,128)S(1)} %fusion.3) | copy-start | bytes 1572868
  252.1 148.4 %all-reduce.3.cloned.1.call-start = ((), (), s32[]{:S(2)}) async-start(), calls=%async_computation.4 | async-start | bytes 2097152 | tf_op jit(solution)/shard_map/psum | solution.py:81
  273.8 11.5 %copy-start.6 = (f32[2,256,256]{2,1,0:T(8,128)S(1)}, f32[2,256,256]{2,1,0:T(8,128)}, u32[]{:S(2)}) copy-start(f32[2,256,256]{2,1,0:T(8,128)} %param.14) | copy-start | bytes 1572868
  281.9 17.1 %collective-permute-start.3 = (f32[2,256,256]{2,1,0:T(8,128)S(1)}, f32[2,256,256]{2,1,0:T(8,128)S(1)}, u32[]{:S(2)}, u32[]{:S(2)}) collective-permute-start(f32[2,256,256]{2,1,0:T(8,128)S(1)} %fusion.1), channel_id=1, source_target_pairs={{0,8},{8,16},{16,24},{24,32},{32,40},{40,48},{48,56},{56,64},{64,7... | collective-permute-start | bytes 1572872 | tf_op jit(solution)/shard_map/ppermute | solution.py:12
  283.8 25.9 %collective-permute-start.1 = (f32[2,256,256]{2,1,0:T(8,128)S(1)}, f32[2,256,256]{2,1,0:T(8,128)S(1)}, u32[]{:S(2)}, u32[]{:S(2)}) collective-permute-start(f32[2,256,256]{2,1,0:T(8,128)S(1)} %fusion.3), channel_id=1, source_target_pairs={{0,8},{8,16},{16,24},{24,32},{32,40},{40,48},{48,56},{56,64},{64,7... | collective-permute-start | bytes 1572872 | tf_op jit(solution)/shard_map/ppermute | solution.py:12
  310.3 10.2 %copy-start.4 = (f32[2,256,256]{2,1,0:T(8,128)}, f32[2,256,256]{2,1,0:T(8,128)S(1)}, u32[]{:S(2)}) copy-start(f32[2,256,256]{2,1,0:T(8,128)S(1)} %fusion.2) | copy-start | bytes 1572868
  317.1 16.4 %collective-permute-start = (f32[2,256,256]{2,1,0:T(8,128)}, f32[2,256,256]{2,1,0:T(8,128)S(1)}, u32[]{:S(2)}, u32[]{:S(2)}) collective-permute-start(f32[2,256,256]{2,1,0:T(8,128)} %convolution_subtract_fusion.1), channel_id=1, source_target_pairs={{0,8},{8,16},{16,24},{24,32},{32,40},{40,48},{48,56},{56,64},{64,7... | collective-permute-start | bytes 1572872 | tf_op jit(solution)/shard_map/ppermute | solution.py:12
  400.5 2.8 copy-start.7
  402.3 1.9 copy-start.5
Sparse Core Ops, SparseCore 0:
  41.5 35.7 all-gather.4
  235.2 38.5 all-gather.6
  276.2 34.6 all-gather.8
  333.7 66.7 all-reduce.2
